TPU v7x, 256 devices: a whole 4x4x8 slice. The times are simulated.
256 devices in a mesh: node: 8 (over z_lo, core), drow: 4 (over x), dcol: 8 (over z_hi, y).
Axes of the slice: x: 4, y: 4, z: 8 (z_hi: 2, z_lo: 4; z = z_hi * 4 + z_lo), core: 2. Of those that a mesh axis runs over, the one named last changes fastest.
Arguments:
- freq_resp: bfloat16 [2, 8, 4096, 8192], P(None, None, ('drow', 'dcol'), 'node'), may hold values from -0.0625 to 0.0625
- node_coords: int32 [2, 8192], P(None, 'node'), may hold values from 0 to 1023
- heading_steps: int32 [2, 512], replicated, may hold values from -8 to 8
- spectral_weights: int32 [8, 512], replicated, may hold values from 1 to 64
Outputs:
- cross_spectra: float32 [2, 8, 4, 1024, 4096], P(None, None, 'drow', 'node', 'dcol')
All inputs are finite; a program needn't handle non-finite values.
Results may differ from a plain program's by a relative error of at most 0.0038.
Values may be sent and summed in bfloat16 or wider, within the bound.
No kernel may reach another device: no remote copies, remote signals or barrier semaphores. Data moves between devices by JAX's collectives and lax.ppermute only.
A program may use at most 128 MiB of HBM per device.

v0:
```python
import math
import jax
import jax.numpy as jnp
from jax import lax
from jax.sharding import PartitionSpec as P

DIRS = 512
FREQS = 8
GRID = 1024


def excitation(coords, heading_steps, spectral_weights):
    freq_index = (jnp.arange(FREQS, dtype=jnp.int32) + 1)[:, None, None]
    project = (
        coords[0][:, None] * heading_steps[0][None, :]
        + coords[1][:, None] * heading_steps[1][None, :]
    )
    turn_count = jnp.mod(freq_index * project[None], GRID)
    phase_angle = turn_count.astype(jnp.float32) * (2.0 * math.pi / GRID)
    spread = jnp.sqrt(spectral_weights.astype(jnp.float32) / (64.0 * DIRS))[:, None, :]
    load_re = (spread * jnp.cos(phase_angle)).astype(jnp.bfloat16)
    load_im = (-spread * jnp.sin(phase_angle)).astype(jnp.bfloat16)
    return (load_re, load_im)


def local(freq_resp, node_coords, heading_steps, spectral_weights):
    load_re, load_im = excitation(node_coords, heading_steps, spectral_weights)
    right_re = jnp.concatenate([load_re, load_im], axis=1)
    right_im = jnp.concatenate([load_im, load_re], axis=1)
    left_re = jnp.concatenate([freq_resp[0], -freq_resp[1]], axis=2)
    left_im = jnp.concatenate([freq_resp[0], freq_resp[1]], axis=2)
    amp_re = jnp.einsum("fkn,fnd->kfd", left_re, right_re, preferred_element_type=jnp.float32)
    amp_im = jnp.einsum("fkn,fnd->kfd", left_im, right_im, preferred_element_type=jnp.float32)
    partial_amp = jnp.stack([amp_re, amp_im], axis=1)
    by_dirs = lax.psum_scatter(partial_amp, "node", scatter_dimension=3, tiled=True).astype(
        jnp.bfloat16
    )
    amplitudes = lax.all_to_all(by_dirs, "node", split_axis=0, concat_axis=3, tiled=True)
    colset = lax.all_gather(amplitudes[None], ("node", "drow"), axis=0, tiled=True)
    col_cat = jnp.concatenate([colset[:, :, 0], colset[:, :, 1]], axis=-1)
    row_piece = lax.all_gather(amplitudes, "dcol", axis=0, tiled=True)
    lead_re = jnp.concatenate([row_piece[:, 0], row_piece[:, 1]], axis=-1)
    lead_im = jnp.concatenate([row_piece[:, 1], -row_piece[:, 0]], axis=-1)
    spec_re = jnp.einsum("kfe,gsfe->fkgs", lead_re, col_cat, preferred_element_type=jnp.float32)
    spec_im = jnp.einsum("kfe,gsfe->fkgs", lead_im, col_cat, preferred_element_type=jnp.float32)
    col_width = spec_re.shape[2] * spec_re.shape[3]
    spec_re = spec_re.reshape(spec_re.shape[0], spec_re.shape[1], col_width)
    spec_im = spec_im.reshape(spec_im.shape[0], spec_im.shape[1], col_width)
    return jnp.stack([spec_re, spec_im], axis=0)[:, :, None]


def solution(mesh):
    placed = (P(None, None, ("drow", "dcol"), "node"), P(None, "node"), P(), P())
    return jax.shard_map(
        local,
        mesh=mesh,
        in_specs=placed,
        out_specs=P(None, None, "drow", "node", "dcol"),
        check_vma=False,
    )
```

profile of v0, /device:TPU:1, one launch (start us, length us, event | category | flops | bytes accessed | tf_op | source)
XLA Modules:
  0.0 401.3 jit_solution(3338056714122250045)
XLA Ops:
  6.5 0.0 reduce-scatter.2.cloned.1.call-start
  6.5 0.0 copy-start
  6.5 0.0 copy-start.4
  6.5 2.8 slice_bitcast_fusion
  9.4 0.6 copy-done
  10.0 0.0 copy-start.5
  10.0 0.0 copy-start.3
  10.0 0.1 fusion.33
  10.1 0.0 copy-done.4
  10.2 0.5 copy-done.5
  10.7 0.0 copy-done.3
  10.7 0.4 multiply_add_fusion
  11.1 71.0 %multiply_convert_fusion = (bf16[8,1024,512]{1,2,0:T(8,128)(2,1)}, bf16[8,1024,512]{1,2,0:T(8,128)(2,1)}) fusion(f32[8,512]{1,0:T(8,128)S(1)} %get-tuple-element.13, s32[1024,512]{0,1:T(8,128)S(1)} %multiply_add_fusion, s32[8]{0:T(128)S(1)} %iota_add_fusion, f32[8,512]{1,0:T(8,128)S(1)} %get-tuple-element.14), kind=kLoop, calls=%fused_computation.16 | loop fusion | flops 75497472 | bytes 18907168 | tf_op jit(solution)/shard_map/convert_element_type | solution.py:22
  82.1 9.2 %fusion.21 = f32[128,1,8,512]{0,3,2,1:T(8,128)} fusion(bf16[8,128,1024]{2,1,0:T(8,128)(2,1)S(1)} %get-tuple-element.8, bf16[8,128,1024]{2,1,0:T(8,128)(2,1)S(1)} %get-tuple-element.7, bf16[8,1024,512]{1,2,0:T(8,128)(2,1)} %get-tuple-element.10, bf16[8,1024,512]{1,2,0:T(8,128)(2,1)} %get-tuple-element.9), kind=kOutput, calls=%fused_computation.40 | convolution fusion | flops 2189426688 | bytes 23068672 | tf_op jit(solution)/shard_map/fkn,fnd->kfd/dot_general | solution.py:33
  91.3 0.0 copy-start.2
  91.3 9.3 %fusion.24 = f32[128,1,8,512]{0,3,2,1:T(8,128)} fusion(bf16[8,128,1024]{2,1,0:T(8,128)(2,1)S(1)} %get-tuple-element.8, bf16[8,128,1024]{2,1,0:T(8,128)(2,1)S(1)} %fusion.33, bf16[8,1024,512]{1,2,0:T(8,128)(2,1)} %get-tuple-element.9, bf16[8,1024,512]{1,2,0:T(8,128)(2,1)} %get-tuple-element.10), kind=kOutput, calls=%fused_computation.41 | convolution fusion | flops 2189426688 | bytes 23068672 | tf_op jit(solution)/shard_map/fkn,fnd->kfd/dot_general | solution.py:32
  100.6 0.0 copy-done.2
  100.6 3.9 pad_maximum_fusion.5
  104.6 0.0 reduce-scatter.2.cloned.1.call-update
  104.6 0.0 all-gather.3.cloned.1.call-start
  104.6 56.8 %reduce-scatter.2.cloned.1.call-done = f32[128,2,8,64]{0,3,2,1:T(8,128)} async-done(((f32[128,2,8,512]{0,3,2,1:T(8,128)}), f32[128,2,8,64]{0,3,2,1:T(8,128)}) %reduce-scatter.2.cloned.1.call-update) | async-done | bytes 524304 | tf_op jit(solution)/shard_map/reduce_scatter | solution.py:35
  161.4 1.1 convert_element_type.19
  162.5 0.4 copy.14
  162.9 0.4 reshape.71
  163.3 14.2 %all_to_all.18 = bf16[8,2,8192]{2,1,0:T(2,128)(2,1)S(1)} all-to-all(bf16[8,2,8192]{2,1,0:T(2,128)(2,1)S(1)} %reshape.71), channel_id=1, replica_groups=mesh['node'=8,'drow'=4,'dcol'=8] {'node'}, dimensions={0} | all-to-all | bytes 524288 | tf_op jit(solution)/shard_map/all_to_all | solution.py:38
  177.5 0.3 reshape.72
  177.9 0.3 copy.15
  178.2 1.0 all_to_all.16
  179.2 0.0 all-gather.3.cloned.1.call-update
  179.3 0.0 all-gather.5.cloned.1.call-start
  179.3 0.6 copy.16
  179.9 1.0 broadcast_in_dim.4
  180.9 0.0 all-gather.5.cloned.1.call-update
  181.0 73.6 %all-gather.3.cloned.1.call-done = bf16[128,2,8,512]{3,0,2,1:T(8,128)(2,1)} async-done(((bf16[16,2,8,512]{3,0,2,1:T(8,128)(2,1)}), bf16[128,2,8,512]{3,0,2,1:T(8,128)(2,1)}) %all-gather.3.cloned.1.call-update) | async-done | bytes 2097168 | tf_op jit(solution)/shard_map/all_gather | solution.py:41
  254.5 1.3 fusion.32
  255.8 1.7 slice_bitcast_fusion.3
  257.6 91.3 %all-gather.5.cloned.1.call-done = bf16[32,16,2,8,512]{4,3,2,1,0:T(8,128)(2,1)} async-done(((bf16[1,16,2,8,512]{4,3,2,1,0:T(8,128)(2,1)}), bf16[32,16,2,8,512]{4,3,2,1,0:T(8,128)(2,1)}) %all-gather.5.cloned.1.call-update) | async-done | bytes 8388624 | tf_op jit(solution)/shard_map/all_gather | solution.py:39
  348.9 3.8 fusion.34
  352.7 11.6 %copy_bitcast_fusion = (bf16[32,16,8,512]{3,0,1,2:T(8,128)(2,1)}, bf16[32,16,8,512]{3,0,1,2:T(8,128)(2,1)}) fusion(bf16[32,16,1,8,512]{4,3,2,1,0:T(8,128)(2,1)S(1)} %get-tuple-element.6, bf16[32,16,1,8,512]{4,3,2,1,0:T(8,128)(2,1)S(1)} %get-tuple-element.5), kind=kLoop, calls=%fused_computation.29 | loop fusion | bytes 16777216 | tf_op jit(solution)/shard_map/squeeze | solution.py:40
  364.2 8.2 %pad_maximum_fusion = bf16[32,16,8,1024]{3,0,1,2:T(8,128)(2,1)} fusion(bf16[32,16,8,512]{3,0,1,2:T(8,128)(2,1)} %get-tuple-element.19, bf16[32,16,8,512]{3,0,1,2:T(8,128)(2,1)} %get-tuple-element.20), kind=kLoop, calls=%fused_computation.18 | loop fusion | flops 16777216 | bytes 16777216 | tf_op jit(solution)/shard_map/concatenate | solution.py:40
  372.4 0.0 copy-start.1
  372.5 10.0 %fusion.13 = f32[8,128,32,16]{1,3,2,0:T(8,128)S(1)} fusion(bf16[32,16,8,1024]{3,0,1,2:T(8,128)(2,1)} %pad_maximum_fusion, bf16[128,8,512]{2,0,1:T(8,128)(2,1)S(1)} %get-tuple-element.12, bf16[128,8,512]{2,0,1:T(8,128)(2,1)S(1)} %get-tuple-element.11), kind=kOutput, calls=%fused_computation.21 | convolution fusion | flops 1077936128 | bytes 12582912 | tf_op jit(solution)/shard_map/kfe,gsfe->fkgs/dot_general | solution.py:44
  382.5 0.0 copy-done.1
  382.5 4.6 %fusion.11 = f32[8,128,32,16]{1,3,2,0:T(8,128)S(1)} fusion(bf16[32,16,8,1024]{3,0,1,2:T(8,128)(2,1)S(1)} %copy-done.1, bf16[128,8,512]{2,0,1:T(8,128)(2,1)S(1)} %fusion.32, bf16[128,8,512]{2,0,1:T(8,128)(2,1)S(1)} %get-tuple-element.12), kind=kOutput, calls=%fused_computation.19 | convolution fusion | flops 1077936128 | bytes 12582912 | tf_op jit(solution)/shard_map/kfe,gsfe->fkgs/dot_general | solution.py:45
  387.1 2.2 maximum_bitcast_fusion
  389.4 5.3 %copy.21 = f32[2,8,1,128,512]{4,3,2,1,0:T(8,128)} copy(f32[2,8,1,128,512]{3,4,1,0,2:T(8,128)} %maximum_bitcast_fusion) | data formatting | bytes 8388608 | tf_op jit(solution)/shard_map/broadcast_in_dim | solution.py:49
  (4 shorter events, 0.0 us)
Async XLA Ops:
  6.5 154.9 %reduce-scatter.2.cloned.1.call-start = ((), (), s32[]{:S(2)}) async-start(), calls=%async_computation.2 | async-start | bytes 4718592 | tf_op jit(solution)/shard_map/reduce_scatter | solution.py:35
  6.5 3.4 copy-start
  6.5 3.6 copy-start.4
  10.0 0.7 copy-start.5
  10.0 0.7 copy-start.3
  91.3 9.3 %copy-start.2 = (f32[128,1,8,512]{0,3,2,1:T(8,128)S(1)}, f32[128,1,8,512]{0,3,2,1:T(8,128)}, u32[]{:S(2)}) copy-start(f32[128,1,8,512]{0,3,2,1:T(8,128)} %fusion.21) | copy-start | bytes 6291460
  104.6 150.0 %all-gather.3.cloned.1.call-start = ((), (), s32[]{:S(2)}) async-start(), calls=%async_computation.3 | async-start | bytes 2359296 | tf_op jit(solution)/shard_map/all_gather | solution.py:41
  179.3 169.6 %all-gather.5.cloned.1.call-start = ((), (), s32[]{:S(2)}) async-start(), calls=%async_computation.4 | async-start | bytes 8650752 | tf_op jit(solution)/shard_map/all_gather | solution.py:39
  372.4 10.0 %copy-start.1 = (bf16[32,16,8,1024]{3,0,1,2:T(8,128)(2,1)S(1)}, bf16[32,16,8,1024]{3,0,1,2:T(8,128)(2,1)}, u32[]{:S(2)}) copy-start(bf16[32,16,8,1024]{3,0,1,2:T(8,128)(2,1)} %pad_maximum_fusion) | copy-start | bytes 25165828
Sparse Core Ops, SparseCore 0:
  104.7 56.6 reduce-scatter.1
  179.4 75.1 all-gather.2
  256.4 92.4 all-gather.4
where the time goes:
time: 402 us; the launch traced here: 401 us
  waiting for transfers between devices  222 us (55%)
  other arithmetic  88.3 us (22%)
  matrix products  33.2 us (8%)
  local copies, waits for them, and re-layouts  30.6 us (8%)
  blocking collectives  14.2 us (4%)
  between operations  13.2 us (3%)
    all_gather x1, waiting for transfers between devices, local(): lax.all_gather(amplitudes[None], ('node', 'drow'), axis=0, tiled=True)  91.3 us
    all_gather x1, waiting for transfers between devices, local(): row_piece = lax.all_gather(amplitudes, 'dcol', axis=0, tiled=True)  73.6 us
    convert_element_type x1, other arithmetic, excitation(): load_im = (-spread * jnp.sin(phase_angle)).astype(jnp.bfloat16)  71 us
    reduce_scatter x1, waiting for transfers between devices, local(): lax.psum_scatter(partial_amp, 'node', scatter_dimension=3, tiled=True)  56.8 us
    all_to_all x1, blocking collectives, local(): lax.all_to_all(by_dirs, 'node', split_axis=0, concat_axis=3, tiled=True)  14.2 us
    squeeze x1, local copies, waits for them, and re-layouts, local(): col_cat = jnp.concatenate([colset[:, :, 0], colset[:, :, 1]], axis=-1)  11.6 us
    dot_general x1, matrix products, local(): jnp.einsum('kfe,gsfe->fkgs', lead_re, col_cat, preferred_element_type=jnp...  10 us
    dot_general x1, matrix products, local(): jnp.einsum('fkn,fnd->kfd', left_re, right_re, preferred_element_type=jnp....  9.32 us
  transfers between devices with their start and end apart: 3, of which 3 were waited for; matrix products, arithmetic and copies ran while one was open for 1% of the time, Pallas kernels for 0%

commit v1 on v0

--- a/solution.py
+++ b/solution.py
@@ -38,7 +38,10 @@
     amplitudes = lax.all_to_all(by_dirs, "node", split_axis=0, concat_axis=3, tiled=True)
     colset = lax.all_gather(amplitudes[None], ("node", "drow"), axis=0, tiled=True)
     col_cat = jnp.concatenate([colset[:, :, 0], colset[:, :, 1]], axis=-1)
-    row_piece = lax.all_gather(amplitudes, "dcol", axis=0, tiled=True)
+    r1 = lax.axis_size("dcol")
+    built = jnp.stack(r1 * [amplitudes])
+    m_next = lax.all_to_all(built, "dcol", split_axis=0, concat_axis=0)
+    row_piece = jnp.concatenate(m_next, 0)
     lead_re = jnp.concatenate([row_piece[:, 0], row_piece[:, 1]], axis=-1)
     lead_im = jnp.concatenate([row_piece[:, 1], -row_piece[:, 0]], axis=-1)
     spec_re = jnp.einsum("kfe,gsfe->fkgs", lead_re, col_cat, preferred_element_type=jnp.float32)

time: 402 us -> 368 us (0.915)
  waiting for transfers between devices: 222 us -> 122 us
  blocking collectives: 14.2 us -> 79 us
    all_gather x1 -> x0, waiting for transfers between devices: 73.6 us -> none  [local(): row_piece = lax.all_gather(amplitudes, 'dcol', axis=0, tiled=True)]
    all_to_all x0 -> x1, blocking collectives: none -> 64.8 us  [local(): m_next = lax.all_to_all(built, 'dcol', split_axis=0, concat_axis=0)]
    all_gather x1, waiting for transfers between devices: 91.3 us -> 65 us  [local(): lax.all_gather(amplitudes[None], ('node', 'drow'), axis=0, tiled=True)]
  transfers between devices with their start and end apart: 3 -> 2, of which waited for: 3 -> 2; matrix products, arithmetic and copies ran while one was open for 1% -> 0% of each run, Pallas kernels for 0% -> 0%
where the time goes in v1:
time: 368 us; the launch traced here: 364 us
  waiting for transfers between devices  122 us (33%)
  other arithmetic  87.1 us (24%)
  blocking collectives  79 us (21%)
  matrix products  33.2 us (9%)
  local copies, waits for them, and re-layouts  28.9 us (8%)
  between operations  13.6 us (4%)
    convert_element_type x1, other arithmetic, excitation(): load_im = (-spread * jnp.sin(phase_angle)).astype(jnp.bfloat16)  71 us
    all_gather x1, waiting for transfers between devices, local(): lax.all_gather(amplitudes[None], ('node', 'drow'), axis=0, tiled=True)  65 us
    all_to_all x1, blocking collectives, local(): m_next = lax.all_to_all(built, 'dcol', split_axis=0, concat_axis=0)  64.8 us
    reduce_scatter x1, waiting for transfers between devices, local(): lax.psum_scatter(partial_amp, 'node', scatter_dimension=3, tiled=True)  56.8 us
    all_to_all x1, blocking collectives, local(): lax.all_to_all(by_dirs, 'node', split_axis=0, concat_axis=3, tiled=True)  14.2 us
    squeeze x1, local copies, waits for them, and re-layouts, local(): col_cat = jnp.concatenate([colset[:, :, 0], colset[:, :, 1]], axis=-1)  11.6 us
    dot_general x1, matrix products, local(): jnp.einsum('kfe,gsfe->fkgs', lead_re, col_cat, preferred_element_type=jnp...  10 us
    dot_general x1, matrix products, local(): jnp.einsum('fkn,fnd->kfd', left_re, right_re, preferred_element_type=jnp....  9.35 us
  transfers between devices with their start and end apart: 2, of which 2 were waited for; matrix products, arithmetic and copies ran while one was open for 0% of the time, Pallas kernels for 0%

profile of v1, /device:TPU:1, one launch (start us, length us, event | category | flops | bytes accessed | tf_op | source)
XLA Modules:
  0.0 363.6 jit_solution(6154898271901964374)
XLA Ops:
  6.5 0.0 reduce-scatter.2.cloned.1.call-start
  6.5 0.0 copy-start
  6.5 0.0 copy-start.4
  6.5 2.8 slice_bitcast_fusion
  9.4 0.6 copy-done
  10.0 0.0 copy-start.5
  10.0 0.0 copy-start.3
  10.0 0.1 fusion.33
  10.1 0.0 copy-done.4
  10.2 0.5 copy-done.5
  10.7 0.0 copy-done.3
  10.7 0.4 multiply_add_fusion
  11.1 71.0 %multiply_convert_fusion = (bf16[8,1024,512]{1,2,0:T(8,128)(2,1)}, bf16[8,1024,512]{1,2,0:T(8,128)(2,1)}) fusion(f32[8,512]{1,0:T(8,128)S(1)} %get-tuple-element.13, s32[1024,512]{0,1:T(8,128)S(1)} %multiply_add_fusion, s32[8]{0:T(128)S(1)} %iota_add_fusion, f32[8,512]{1,0:T(8,128)S(1)} %get-tuple-element.14), kind=kLoop, calls=%fused_computation.16 | loop fusion | flops 75497472 | bytes 18907168 | tf_op jit(solution)/shard_map/convert_element_type | solution.py:22
  82.1 9.2 %fusion.21 = f32[128,1,8,512]{0,3,2,1:T(8,128)} fusion(bf16[8,128,1024]{2,1,0:T(8,128)(2,1)S(1)} %get-tuple-element.8, bf16[8,128,1024]{2,1,0:T(8,128)(2,1)S(1)} %get-tuple-element.7, bf16[8,1024,512]{1,2,0:T(8,128)(2,1)} %get-tuple-element.10, bf16[8,1024,512]{1,2,0:T(8,128)(2,1)} %get-tuple-element.9), kind=kOutput, calls=%fused_computation.40 | convolution fusion | flops 2189426688 | bytes 23068672 | tf_op jit(solution)/shard_map/fkn,fnd->kfd/dot_general | solution.py:33
  91.3 0.0 copy-start.2
  91.3 9.4 %fusion.24 = f32[128,1,8,512]{0,3,2,1:T(8,128)} fusion(bf16[8,128,1024]{2,1,0:T(8,128)(2,1)S(1)} %get-tuple-element.8, bf16[8,128,1024]{2,1,0:T(8,128)(2,1)S(1)} %fusion.33, bf16[8,1024,512]{1,2,0:T(8,128)(2,1)} %get-tuple-element.9, bf16[8,1024,512]{1,2,0:T(8,128)(2,1)} %get-tuple-element.10), kind=kOutput, calls=%fused_computation.41 | convolution fusion | flops 2189426688 | bytes 23068672 | tf_op jit(solution)/shard_map/fkn,fnd->kfd/dot_general | solution.py:32
  100.7 0.0 copy-done.2
  100.7 3.9 %pad_maximum_fusion.5 = f32[128,2,8,512]{0,3,2,1:T(8,128)} fusion(f32[128,1,8,512]{0,3,2,1:T(8,128)S(1)} %copy-done.2, f32[128,1,8,512]{0,3,2,1:T(8,128)} %fusion.24), kind=kLoop, calls=%fused_computation.27 | loop fusion | flops 1048576 | bytes 8388608 | tf_op jit(solution)/shard_map/stack | solution.py:34
  104.6 0.0 reduce-scatter.2.cloned.1.call-update
  104.6 0.0 all-gather.2.cloned.1.call-start
  104.7 56.8 %reduce-scatter.2.cloned.1.call-done = f32[128,2,8,64]{0,3,2,1:T(8,128)} async-done(((f32[128,2,8,512]{0,3,2,1:T(8,128)}), f32[128,2,8,64]{0,3,2,1:T(8,128)}) %reduce-scatter.2.cloned.1.call-update) | async-done | bytes 524304 | tf_op jit(solution)/shard_map/reduce_scatter | solution.py:35
  161.4 1.1 convert_element_type.19
  162.5 0.4 copy.14
  163.0 0.4 reshape.78
  163.4 14.2 %all_to_all.20 = bf16[8,2,8192]{2,1,0:T(2,128)(2,1)S(1)} all-to-all(bf16[8,2,8192]{2,1,0:T(2,128)(2,1)S(1)} %reshape.78), channel_id=1, replica_groups=mesh['node'=8,'drow'=4,'dcol'=8] {'node'}, dimensions={0} | all-to-all | bytes 524288 | tf_op jit(solution)/shard_map/all_to_all | solution.py:38
  177.6 0.3 reshape.79
  177.9 0.6 copy.15
  178.5 1.0 stack.32
  179.6 0.0 all-gather.2.cloned.1.call-update
  179.6 0.3 copy.29
  179.9 0.3 reshape.77
  180.3 0.3 stack.31
  180.5 64.8 %all_to_all.21 = bf16[8,16,2,8,512]{4,1,3,2,0:T(8,128)(2,1)S(1)} all-to-all(bf16[8,16,2,8,512]{4,1,3,2,0:T(8,128)(2,1)S(1)} %stack.31), channel_id=1, replica_groups=mesh['node'=8,'drow'=4,'dcol'=8] {'dcol'}, dimensions={0} | all-to-all | bytes 4194304 | tf_op jit(solution)/shard_map/all_to_all | solution.py:43
  245.3 0.2 copy.17
  245.6 0.1 fusion.32
  245.6 0.2 slice_bitcast_fusion.3
  245.9 65.0 %all-gather.2.cloned.1.call-done = bf16[32,16,2,8,512]{4,3,2,1,0:T(8,128)(2,1)} async-done(((bf16[1,16,2,8,512]{4,3,2,1,0:T(8,128)(2,1)}), bf16[32,16,2,8,512]{4,3,2,1,0:T(8,128)(2,1)}) %all-gather.2.cloned.1.call-update) | async-done | bytes 8388624 | tf_op jit(solution)/shard_map/all_gather | solution.py:39
  310.9 3.8 %fusion.34 = (bf16[32,16,1,8,512]{4,3,2,1,0:T(8,128)(2,1)S(1)}, bf16[32,16,1,8,512]{4,3,2,1,0:T(8,128)(2,1)S(1)}) fusion(bf16[32,16,2,8,512]{4,3,2,1,0:T(8,128)(2,1)} %all-gather.2.cloned.1.call-done), kind=kLoop, calls=%fused_computation.53 | loop fusion | bytes 16777216 | tf_op jit(solution)/shard_map/slice | solution.py:40
  314.7 11.6 %copy_bitcast_fusion = (bf16[32,16,8,512]{3,0,1,2:T(8,128)(2,1)}, bf16[32,16,8,512]{3,0,1,2:T(8,128)(2,1)}) fusion(bf16[32,16,1,8,512]{4,3,2,1,0:T(8,128)(2,1)S(1)} %get-tuple-element.6, bf16[32,16,1,8,512]{4,3,2,1,0:T(8,128)(2,1)S(1)} %get-tuple-element.5), kind=kLoop, calls=%fused_computation.29 | loop fusion | bytes 16777216 | tf_op jit(solution)/shard_map/squeeze | solution.py:40
  326.3 8.2 %pad_maximum_fusion = bf16[32,16,8,1024]{3,0,1,2:T(8,128)(2,1)} fusion(bf16[32,16,8,512]{3,0,1,2:T(8,128)(2,1)} %get-tuple-element.19, bf16[32,16,8,512]{3,0,1,2:T(8,128)(2,1)} %get-tuple-element.20), kind=kLoop, calls=%fused_computation.18 | loop fusion | flops 16777216 | bytes 16777216 | tf_op jit(solution)/shard_map/concatenate | solution.py:40
  334.5 0.0 copy-start.1
  334.5 10.0 %fusion.13 = f32[8,128,32,16]{1,3,2,0:T(8,128)S(1)} fusion(bf16[32,16,8,1024]{3,0,1,2:T(8,128)(2,1)} %pad_maximum_fusion, bf16[128,8,512]{2,0,1:T(8,128)(2,1)S(1)} %get-tuple-element.12, bf16[128,8,512]{2,0,1:T(8,128)(2,1)S(1)} %get-tuple-element.11), kind=kOutput, calls=%fused_computation.21 | convolution fusion | flops 1077936128 | bytes 12582912 | tf_op jit(solution)/shard_map/kfe,gsfe->fkgs/dot_general | solution.py:47
  344.5 0.0 copy-done.1
  344.5 4.6 %fusion.11 = f32[8,128,32,16]{1,3,2,0:T(8,128)S(1)} fusion(bf16[32,16,8,1024]{3,0,1,2:T(8,128)(2,1)S(1)} %copy-done.1, bf16[128,8,512]{2,0,1:T(8,128)(2,1)S(1)} %fusion.32, bf16[128,8,512]{2,0,1:T(8,128)(2,1)S(1)} %get-tuple-element.12), kind=kOutput, calls=%fused_computation.19 | convolution fusion | flops 1077936128 | bytes 12582912 | tf_op jit(solution)/shard_map/kfe,gsfe->fkgs/dot_general | solution.py:48
  349.2 2.3 maximum_bitcast_fusion
  351.5 5.3 %copy.23 = f32[2,8,1,128,512]{4,3,2,1,0:T(8,128)} copy(f32[2,8,1,128,512]{3,4,1,0,2:T(8,128)} %maximum_bitcast_fusion) | data formatting | bytes 8388608 | tf_op jit(solution)/shard_map/broadcast_in_dim | solution.py:52
  (4 shorter events, 0.0 us)
Async XLA Ops:
  6.5 154.9 %reduce-scatter.2.cloned.1.call-start = ((), (), s32[]{:S(2)}) async-start(), calls=%async_computation.3 | async-start | bytes 4718592 | tf_op jit(solution)/shard_map/reduce_scatter | solution.py:35
  6.5 3.4 copy-start
  6.5 3.6 copy-start.4
  10.0 0.7 copy-start.5
  10.0 0.7 copy-start.3
  91.3 9.4 %copy-start.2 = (f32[128,1,8,512]{0,3,2,1:T(8,128)S(1)}, f32[128,1,8,512]{0,3,2,1:T(8,128)}, u32[]{:S(2)}) copy-start(f32[128,1,8,512]{0,3,2,1:T(8,128)} %fusion.21) | copy-start | bytes 6291460
  104.6 206.3 %all-gather.2.cloned.1.call-start = ((), (), s32[]{:S(2)}) async-start(), calls=%async_computation.4 | async-start | bytes 8650752 | tf_op jit(solution)/shard_map/all_gather | solution.py:39
  334.5 10.1 %copy-start.1 = (bf16[32,16,8,1024]{3,0,1,2:T(8,128)(2,1)S(1)}, bf16[32,16,8,1024]{3,0,1,2:T(8,128)(2,1)}, u32[]{:S(2)}) copy-start(bf16[32,16,8,1024]{3,0,1,2:T(8,128)(2,1)} %pad_maximum_fusion) | copy-start | bytes 25165828
Sparse Core Ops, SparseCore 0:
  104.7 56.6 reduce-scatter.1
  179.7 131.1 all-gather.1
